TPU v7x, 512 devices: a whole 4x4x16 slice. The times are simulated.
512 devices in a mesh: ctx: 32 (over z_hi, y, x), exp: 16 (over z_lo, core).
Axes of the slice: x: 4, y: 4, z: 16 (z_hi: 2, z_lo: 8; z = z_hi * 8 + z_lo), core: 2. Of those that a mesh axis runs over, the one named last changes fastest.
Arguments:
- hidden_in: bfloat16 [4096, 2880], P('ctx'), may hold values from -6 to 6
- query_input: bfloat16 [4096, 2048], P('ctx', 'exp'), may hold values from -16 to 16
- key_heads_input: bfloat16 [4096, 256], P('ctx'), may hold values from -16 to 16
- value_heads_input: bfloat16 [4096, 256], P('ctx'), may hold values from -6 to 6
- sink_logits: float32 [32], P('exp'), may hold values from 0 to 4
- out_proj: bfloat16 [2048, 2880], P('exp'), may hold values from -0.125 to 0.125
- norm_gain: float32 [2880], replicated, may hold values from 0.5 to 1.5
- expert_ids: int32 [4096, 4], P('ctx'), may hold values from 0 to 31, all different within a row; in each aligned block of 128 rows (0 to 127, 128 to 255, ...) at most 20 rows name the same one
- expert_gates: float32 [4096, 4], P('ctx'), may hold values from 0.1 to 1
- gate_up: bfloat16 [32, 2880, 2, 2880], P('ctx', None, None, 'exp'), may hold values from -0.109375 to 0.109375
- down_proj: bfloat16 [32, 2880, 2880], P('ctx', 'exp'), may hold values from -0.109375 to 0.109375
Outputs:
- layer_out: bfloat16 [4096, 2880], P('ctx', 'exp')
Inputs may be any that keep to these rules, and one draw needn't show every extreme that they name: `expert_ids`: each token names 4 different experts; within the 128 tokens of one device no expert is named by more than 20 tokens.
All inputs are finite; a program needn't handle non-finite values.
Results may differ from a plain program's by a relative error of at most 0.02.
Values may be sent and summed in bfloat16 or wider, within the bound.
No kernel may reach another device: no remote copies, remote signals or barrier semaphores. Data moves between devices by JAX's collectives and lax.ppermute only.
A program may use at most 64 MiB of HBM per device.

v0:
```python
import functools
import math
import jax
import jax.numpy as jnp
import numpy as np
from jax import lax
from jax.sharding import Mesh, PartitionSpec as P

D = 2880
QUERY_HEADS = 32
KEY_VALUE_HEADS = 4
HEAD_SIZE = 64
yarn_base = 150000.0
yarn_factor = 32.0
yarn_initial = 4096.0
beta_fast = 32.0
beta_slow = 1.0
neg_large = -1e30


def yarn_frequencies(head_dim):
    half_dim = head_dim // 2

    def correction(rotations):
        return (
            head_dim
            * math.log(yarn_initial / (rotations * 2.0 * math.pi))
            / (2.0 * math.log(yarn_base))
        )

    lower_dim = max(math.floor(correction(beta_fast)), 0)
    upper_dim = min(math.ceil(correction(beta_slow)), head_dim - 1)
    extrap_freq = 1.0 / yarn_base ** (np.arange(0, head_dim, 2) / head_dim)
    interp_freq = extrap_freq / yarn_factor
    ramp_part = np.clip((np.arange(half_dim) - lower_dim) / (upper_dim - lower_dim), 0.0, 1.0)
    extrap_share = 1.0 - ramp_part
    return (interp_freq * (1.0 - extrap_share) + extrap_freq * extrap_share).astype(np.float32)


def rotate_with_yarn(heads_in, token_positions):
    head_dim = heads_in.shape[-1]
    freqs = jnp.asarray(yarn_frequencies(head_dim))
    angles = token_positions.astype(jnp.float32)[:, None] * freqs[None, :]
    factor = 0.1 * math.log(yarn_factor) + 1.0
    cosine = (jnp.cos(angles) * factor)[:, None, :]
    sine = (jnp.sin(angles) * factor)[:, None, :]
    first_half = heads_in[..., : head_dim // 2]
    second_half = heads_in[..., head_dim // 2 :]
    return jnp.concatenate(
        [first_half * cosine - second_half * sine, second_half * cosine + first_half * sine],
        axis=-1,
    )


def route_slots(ids_block, n_experts):
    flat_ids = ids_block.reshape(-1)
    onehot = (flat_ids[:, None] == jnp.arange(n_experts, dtype=jnp.int32)[None, :]).astype(
        jnp.int32
    )
    ranks = jnp.cumsum(onehot, axis=0) - onehot
    return jnp.sum(ranks * onehot, axis=1).reshape(ids_block.shape)


CTX = ("zh", "y", "x")
EXP = ("zl", "c")


def per_device(
    hidden_in,
    query_input,
    key_heads_input,
    value_heads_input,
    sink_logits,
    out_proj,
    norm_gain,
    expert_ids,
    expert_gates,
    gate_up,
    down_proj,
    *,
    ctx_count,
    zl_count,
    c_count
):
    tok_rows = hidden_in.shape[0]
    exp_count = zl_count * c_count
    local_heads = query_input.shape[1] // HEAD_SIZE
    ctx_index = lax.axis_index(CTX)
    exp_index = lax.axis_index(EXP)
    token_positions = ctx_index * tok_rows + jnp.arange(tok_rows, dtype=jnp.int32)
    q_rot = rotate_with_yarn(
        query_input.astype(jnp.float32).reshape(tok_rows, local_heads, HEAD_SIZE), token_positions
    ).astype(jnp.bfloat16)
    shared_key_head = exp_index * local_heads // (QUERY_HEADS // KEY_VALUE_HEADS)
    key_block = lax.dynamic_slice_in_dim(key_heads_input, shared_key_head * HEAD_SIZE, HEAD_SIZE, 1)
    value_block = lax.dynamic_slice_in_dim(
        value_heads_input, shared_key_head * HEAD_SIZE, HEAD_SIZE, 1
    )
    key_rot = (
        rotate_with_yarn(
            key_block.astype(jnp.float32).reshape(tok_rows, 1, HEAD_SIZE), token_positions
        )
        .reshape(tok_rows, HEAD_SIZE)
        .astype(jnp.bfloat16)
    )
    key_value = jnp.concatenate([key_rot, value_block], axis=1)
    score_scale = 1.0 / math.sqrt(HEAD_SIZE)
    block_part = lax.all_gather(key_value, CTX, axis=0, tiled=True)
    run_max = jnp.broadcast_to(sink_logits[:, None], (local_heads, tok_rows))
    run_total = jnp.ones((local_heads, tok_rows), jnp.float32)
    key_count = block_part.shape[0]
    key_part = block_part[:, :HEAD_SIZE]
    value_part = block_part[:, HEAD_SIZE:].astype(jnp.float32)
    scores = (
        jnp.einsum("rhd,kd->hrk", q_rot, key_part, preferred_element_type=jnp.float32) * score_scale
    )
    key_pos = jnp.arange(key_count, dtype=jnp.int32)
    visible = token_positions[:, None] >= key_pos[None, :]
    scores = jnp.where(visible[None, :, :], scores, neg_large)
    new_max = jnp.maximum(run_max, jnp.max(scores, axis=2))
    weights = jnp.exp(scores - new_max[:, :, None])
    factor = jnp.exp(run_max - new_max)
    run_total = run_total * factor + jnp.sum(weights, axis=2)
    run_sum = jnp.einsum("hrk,kd->hrd", weights, value_part, precision=lax.Precision.HIGHEST)
    attended = (
        (run_sum / run_total[:, :, None])
        .transpose(1, 0, 2)
        .reshape(tok_rows, local_heads * HEAD_SIZE)
        .astype(jnp.bfloat16)
    )
    col_width = D // exp_count
    head_part = jnp.dot(attended, out_proj, preferred_element_type=jnp.float32).astype(jnp.bfloat16)
    head_part = head_part.reshape(tok_rows, zl_count, c_count, col_width).transpose(2, 1, 0, 3)
    head_part = lax.psum_scatter(head_part, "c", scatter_dimension=0, tiled=True)[0]
    head_cols = lax.psum_scatter(head_part, "zl", scatter_dimension=0, tiled=True)[0]
    residual_cols = lax.dynamic_slice_in_dim(hidden_in, exp_index * col_width, col_width, 1).astype(
        jnp.float32
    ) + head_cols.astype(jnp.float32)
    square_sum = lax.psum(jnp.sum(residual_cols * residual_cols, axis=1), EXP)
    gain_cols = lax.dynamic_slice_in_dim(norm_gain, exp_index * col_width, col_width, 0)
    normed_cols = (
        residual_cols * lax.rsqrt(square_sum / D + 1e-05)[:, None] * gain_cols[None, :]
    ).astype(jnp.bfloat16)
    exp_local = gate_up.shape[0]
    n_experts = exp_local * ctx_count
    top_count = expert_ids.shape[1]
    capacity = max(2, tok_rows * top_count * 5 // (4 * n_experts))
    slot_index = route_slots(expert_ids, n_experts)
    dest_row = expert_ids * capacity + slot_index
    spread_rows = jnp.broadcast_to(
        normed_cols[:, None, :], (tok_rows, top_count, col_width)
    ).reshape(tok_rows * top_count, col_width)
    send_rows = (
        jnp.zeros((n_experts * capacity, col_width), jnp.bfloat16)
        .at[dest_row.reshape(-1)]
        .set(spread_rows)
    )
    bucket_rows = ctx_count * capacity
    unit_count = gate_up.shape[-1]
    received = lax.all_to_all(
        send_rows.reshape(ctx_count, exp_local * capacity, col_width),
        CTX,
        split_axis=0,
        concat_axis=0,
        tiled=True,
    ).reshape(bucket_rows, col_width)
    gathered = lax.all_gather(received, "zl", axis=0, tiled=False)
    gathered = lax.all_gather(gathered, "c", axis=0, tiled=False)
    weights_flat = gate_up.reshape(zl_count, c_count, col_width, 2 * unit_count)
    gate_up_out = jnp.einsum(
        "czrk,zckf->rf", gathered, weights_flat, preferred_element_type=jnp.float32
    )
    gate_up_out = gate_up_out.reshape(bucket_rows, 2, unit_count)
    gate_value = gate_up_out[:, 0]
    up_value = gate_up_out[:, 1]
    activated = ((up_value + 1.0) * gate_value * jax.nn.sigmoid(1.702 * gate_value)).astype(
        jnp.bfloat16
    )
    down_local = down_proj.reshape(unit_count, zl_count, c_count, col_width)
    partial_value = jnp.einsum(
        "rf,fzcd->czrd", activated, down_local, preferred_element_type=jnp.float32
    ).astype(jnp.bfloat16)
    partial_value = lax.psum_scatter(partial_value, "c", scatter_dimension=0, tiled=True)[0]
    expert_cols = lax.psum_scatter(partial_value, "zl", scatter_dimension=0, tiled=True)[0]
    returned = lax.all_to_all(
        expert_cols.reshape(ctx_count, capacity, col_width),
        CTX,
        split_axis=0,
        concat_axis=0,
        tiled=True,
    )
    picked_rows = returned.reshape(n_experts * capacity, col_width)[dest_row]
    moe_cols = jnp.sum(expert_gates[:, :, None] * picked_rows.astype(jnp.float32), axis=1)
    return (residual_cols + moe_cols).astype(jnp.bfloat16)


def solution(mesh):
    ctx_count, exp_count = mesh.devices.shape
    zh, y, x = (mesh.devices.shape[0] // 16, 4, 4)
    c_count = 2
    zl_count = exp_count // c_count
    fine = Mesh(mesh.devices.reshape(zh, y, x, zl_count, c_count), ("zh", "y", "x", "zl", "c"))
    placed = (
        P(CTX, None),
        P(CTX, EXP),
        P(CTX, None),
        P(CTX, None),
        P(EXP),
        P(EXP, None),
        P(),
        P(CTX, None),
        P(CTX, None),
        P(CTX, None, None, EXP),
        P(CTX, EXP, None),
    )
    return jax.shard_map(
        functools.partial(per_device, ctx_count=ctx_count, zl_count=zl_count, c_count=c_count),
        mesh=fine,
        in_specs=placed,
        out_specs=P(CTX, EXP),
        check_vma=False,
    )
```

profile of v0, /device:TPU:32, one launch (start us, length us, event | category | flops | bytes accessed | tf_op | source)
XLA Modules:
  0.0 534.8 jit_solution(13582523231836904942)
XLA Ops:
  11.3 113.0 %all-gather.5.cloned.1.call-done = bf16[4096,128]{0,1:T(8,128)(2,1)} async-done(((bf16[128,128]{0,1:T(8,128)(2,1)}), bf16[4096,128]{0,1:T(8,128)(2,1)}) %all-gather.5.cloned.1.call-update) | async-done | bytes 1048592 | tf_op jit(solution)/shard_map/all_gather | solution.py:108
  124.3 2.0 fusion.45
  127.0 2.1 fusion.13
  131.1 16.4 %reduce-scatter.11.cloned.1.call-done = bf16[1,8,128,180]{2,1,3,0:T(8,128)(2,1)} async-done(((bf16[2,8,128,180]{2,1,3,0:T(8,128)(2,1)}), bf16[1,8,128,180]{2,1,3,0:T(8,128)(2,1)}) %reduce-scatter.11.cloned.1.call-update) | async-done | bytes 368656 | tf_op jit(solution)/shard_map/reduce_scatter | solution.py:134
  153.0 55.7 %reduce-scatter.15.cloned.1.call-done = bf16[1,128,180]{1,2,0:T(8,128)(2,1)} async-done(((bf16[8,128,180]{1,2,0:T(8,128)(2,1)}), bf16[1,128,180]{1,2,0:T(8,128)(2,1)}) %reduce-scatter.15.cloned.1.call-update) | async-done | bytes 46096
  209.7 44.4 %psum.7 = f32[128]{0:T(128)S(1)} all-reduce(f32[128]{0:T(128)S(1)} %multiply_reduce_fusion.1), channel_id=1, replica_groups=mesh['zh'=2,'y'=4,'x'=4,'zl'=8,'c'=2] {'zl','c'}, use_global_device_ids=true, to_apply=%region_8.9 | all-reduce | flops 128 | bytes 1024 | tf_op jit(solution)/shard_map/psum | solution.py:139
  254.4 2.4 scatter_custom_fusion
  256.9 30.0 %all_to_all.10 = bf16[32,20,180]{2,1,0:T(8,128)(2,1)S(1)} all-to-all(bf16[32,20,180]{2,1,0:T(8,128)(2,1)S(1)} %reshape.312), channel_id=1, replica_groups=mesh['zh'=2,'y'=4,'x'=4,'zl'=8,'c'=2] {'zh','y','x'}, dimensions={0} | all-to-all | bytes 460800 | tf_op jit(solution)/shard_map/all_to_all | solution.py:160
  288.0 62.0 %all-gather.7.cloned.1.call-done = bf16[8,640,180]{1,2,0:T(8,128)(2,1)} async-done(((bf16[1,640,180]{1,2,0:T(8,128)(2,1)}), bf16[8,640,180]{1,2,0:T(8,128)(2,1)}) %all-gather.7.cloned.1.call-update) | async-done | bytes 1843216 | tf_op jit(solution)/shard_map/all_gather | solution.py:167
  349.9 3.0 copy.79
  353.2 1.8 copy.81
  355.0 9.8 %reshape.313 = bf16[8,2,180,360]{2,1,0,3:T(2,128)(2,1)} reshape(bf16[1,2880,2,180]{1,3,2,0:T(8,128)(2,1)S(1)} %copy.81) | data formatting | bytes 4147200 | tf_op jit(solution)/shard_map/reshape | solution.py:169
  364.8 6.4 %reshape.314 = bf16[180,8,2,180]{3,2,1,0:T(2,128)(2,1)S(1)} reshape(bf16[1,180,2880]{2,1,0:T(8,128)(2,1)} %param.23) | data formatting | bytes 2073600 | tf_op jit(solution)/shard_map/reshape | solution.py:179
  371.2 5.6 %all-gather.9.cloned.1.call-done = bf16[16,640,180]{1,0,2:T(8,128)(2,1)} async-done(((bf16[8,640,180]{1,0,2:T(8,128)(2,1)}), bf16[16,640,180]{1,0,2:T(8,128)(2,1)}) %all-gather.9.cloned.1.call-update) | async-done | bytes 3686416 | tf_op jit(solution)/shard_map/all_gather | solution.py:168
  376.8 3.0 copy.80
  379.8 3.0 fusion.8
  382.9 1.8 convert_bitcast_fusion
  384.7 2.6 copy.85
  387.5 23.2 %reduce-scatter.13.cloned.1.call-done = bf16[1,8,640,180]{2,1,3,0:T(8,128)(2,1)} async-done(((bf16[2,8,640,180]{2,1,3,0:T(8,128)(2,1)}), bf16[1,8,640,180]{2,1,3,0:T(8,128)(2,1)}) %reduce-scatter.13.cloned.1.call-update) | async-done | bytes 1843216 | tf_op jit(solution)/shard_map/reduce_scatter | solution.py:183
  410.8 3.0 copy.86
  413.8 69.3 %reduce-scatter.17.cloned.1.call-done = bf16[1,640,180]{1,2,0:T(8,128)(2,1)} async-done(((bf16[8,640,180]{1,2,0:T(8,128)(2,1)}), bf16[1,640,180]{1,2,0:T(8,128)(2,1)}) %reduce-scatter.17.cloned.1.call-update) | async-done | bytes 230416
  485.0 17.0 %all-to-all-start.1 = ((bf16[32,20,180]{2,1,0:T(8,128)(2,1)}), bf16[32,20,180]{2,1,0:T(8,128)(2,1)S(1)}, u32[]{:S(2)}, u32[]{:S(2)}) async-start(bf16[32,20,180]{2,1,0:T(8,128)(2,1)} %reshape_squeeze.3), calls=%async_computation.3 | async-start | bytes 786432 | tf_op jit(solution)/shard_map/all_to_all | solution.py:185
  502.3 22.2 %all-to-all-done.1 = bf16[32,20,180]{2,1,0:T(8,128)(2,1)S(1)} async-done(((bf16[32,20,180]{2,1,0:T(8,128)(2,1)}), bf16[32,20,180]{2,1,0:T(8,128)(2,1)S(1)}, u32[]{:S(2)}, u32[]{:S(2)}) %all-to-all-start.1) | async-done | bytes 230432 | tf_op jit(solution)/shard_map/all_to_all | solution.py:185
  524.6 2.0 gather_fusion
  (84 shorter events, 19.4 us)
Async XLA Ops:
  6.5 122.5 %copy-start = (bf16[128,2880]{0,1:T(8,128)(2,1)S(1)}, bf16[128,2880]{0,1:T(8,128)(2,1)}, u32[]{:S(2)}) copy-start(bf16[128,2880]{0,1:T(8,128)(2,1)} %param.18) | copy-start | bytes 2211844
  6.5 119.7 %copy-start.5 = (f32[2]{0:T(128)S(1)}, f32[2]{0:T(128)}, u32[]{:S(2)}) copy-start(f32[2]{0:T(128)} %param.17) | copy-start | bytes 28
  6.5 117.7 %all-gather.5.cloned.1.call-start = ((), (), s32[]{:S(2)}) async-start(), calls=%async_computation.6 | async-start | bytes 1081344 | tf_op jit(solution)/shard_map/all_gather | solution.py:108
  9.2 138.3 %reduce-scatter.11.cloned.1.call-start = ((), (), s32[]{:S(2)}) async-start(), calls=%async_computation.7 | async-start | bytes 1105920 | tf_op jit(solution)/shard_map/reduce_scatter | solution.py:134
  124.3 2.7 copy-start.2
  129.1 1.6 copy-start.3
  130.7 78.0 %reduce-scatter.15.cloned.1.call-start = ((), (), s32[]{:S(2)}) async-start(), calls=%async_computation.11 | async-start | bytes 423936
  149.3 200.7 %all-gather.7.cloned.1.call-start = ((), (), s32[]{:S(2)}) async-start(), calls=%async_computation.8 | async-start | bytes 2119680 | tf_op jit(solution)/shard_map/all_gather | solution.py:167
  287.9 88.9 %all-gather.9.cloned.1.call-start = ((), (), s32[]{:S(2)}) async-start(), calls=%async_computation.10 | async-start | bytes 5529600 | tf_op jit(solution)/shard_map/all_gather | solution.py:168
  353.0 57.8 %reduce-scatter.13.cloned.1.call-start = ((), (), s32[]{:S(2)}) async-start(), calls=%async_computation.9 | async-start | bytes 5529600 | tf_op jit(solution)/shard_map/reduce_scatter | solution.py:183
  376.8 3.0 copy-start.1
  387.3 95.8 %reduce-scatter.17.cloned.1.call-start = ((), (), s32[]{:S(2)}) async-start(), calls=%async_computation.12 | async-start | bytes 2119680
  410.8 91.4 %copy-start.4 = (f32[128,4]{0,1:T(4,128)S(1)}, f32[128,4]{0,1:T(4,128)}, u32[]{:S(2)}) copy-start(f32[128,4]{0,1:T(4,128)} %param.21) | copy-start | bytes 6148
  485.0 39.5 %all-to-all-start.1 = ((bf16[32,20,180]{2,1,0:T(8,128)(2,1)}), bf16[32,20,180]{2,1,0:T(8,128)(2,1)S(1)}, u32[]{:S(2)}, u32[]{:S(2)}) async-start(bf16[32,20,180]{2,1,0:T(8,128)(2,1)} %reshape_squeeze.3), calls=%async_computation.3 | async-start | bytes 786432 | tf_op jit(solution)/shard_map/all_to_all | solution.py:185
Sparse Core Ops, SparseCore 0:
  11.4 112.7 all-gather.4
  130.8 16.6 reduce-scatter.10
  150.3 58.3 reduce-scatter.14
  288.1 61.8 all-gather.6
  353.1 23.7 all-gather.8
  387.4 23.3 reduce-scatter.12
  413.9 69.0 reduce-scatter.16
where the time goes:
time: 535 us
  waiting for transfers between devices  367 us (69%)
  blocking collectives  74.4 us (14%)
  local copies, waits for them, and re-layouts  46.9 us (9%)
  starting transfers between devices  17.6 us (3%)
  between operations  13.8 us (3%)
  matrix products  9.28 us (2%)
    unnamed x9, waiting for transfers between devices  125 us
    all_gather x1, waiting for transfers between devices, per_device(): block_part = lax.all_gather(key_value, CTX, axis=0, tiled=True)  113 us
    all_gather x1, waiting for transfers between devices, per_device(): gathered = lax.all_gather(received, 'zl', axis=0, tiled=False)  62 us
    psum x1, blocking collectives, per_device(): square_sum = lax.psum(jnp.sum(residual_cols * residual_cols, axis=1), EXP)  44.4 us
    all_to_all x1, blocking collectives, per_device(): lax.all_to_all(send_rows.reshape(ctx_count, exp_local * capacity, col_wid...  30 us
    reduce_scatter x1, waiting for transfers between devices, per_device(): lax.psum_scatter(partial_value, 'c', scatter_dimension=0, tiled=True)[0]  23.2 us
    all_to_all x1, waiting for transfers between devices, per_device(): lax.all_to_all(expert_cols.reshape(ctx_count, capacity, col_width), CTX,...  22.2 us
    all_to_all x1, starting transfers between devices, per_device(): lax.all_to_all(expert_cols.reshape(ctx_count, capacity, col_width), CTX,...  17 us
  transfers between devices with their start and end apart: 8, of which 8 were waited for; matrix products, arithmetic and copies ran while one was open for 5% of the time, Pallas kernels for 0%

commit v1 on v0

--- a/solution.py
+++ b/solution.py
@@ -136,7 +136,9 @@
     residual_cols = lax.dynamic_slice_in_dim(hidden_in, exp_index * col_width, col_width, 1).astype(
         jnp.float32
     ) + head_cols.astype(jnp.float32)
-    square_sum = lax.psum(jnp.sum(residual_cols * residual_cols, axis=1), EXP)
+    square_sum = jnp.sum(
+        lax.all_gather(jnp.sum(residual_cols * residual_cols, axis=1), EXP), axis=0
+    )
     gain_cols = lax.dynamic_slice_in_dim(norm_gain, exp_index * col_width, col_width, 0)
     normed_cols = (
         residual_cols * lax.rsqrt(square_sum / D + 1e-05)[:, None] * gain_cols[None, :]

time: 535 us -> 529 us (0.989)
  blocking collectives: 74.4 us -> 64.5 us
    psum x1 -> x0, blocking collectives: 44.4 us -> none  [per_device(): square_sum = lax.psum(jnp.sum(residual_cols * residual_cols, axis=1), EXP)]
    all_gather x0 -> x1, blocking collectives: none -> 32.9 us  [per_device(): lax.all_gather(jnp.sum(residual_cols * residual_cols, axis=1), EXP)]
where the time goes in v1:
time: 529 us
  waiting for transfers between devices  371 us (70%)
  blocking collectives  64.5 us (12%)
  local copies, waits for them, and re-layouts  46.9 us (9%)
  starting transfers between devices  17.6 us (3%)
  between operations  13.8 us (3%)
  matrix products  9.28 us (2%)
  other arithmetic  5.31 us (1%)
    unnamed x9, waiting for transfers between devices  125 us
    all_gather x1, waiting for transfers between devices, per_device(): block_part = lax.all_gather(key_value, CTX, axis=0, tiled=True)  113 us
    all_gather x1, waiting for transfers between devices, per_device(): gathered = lax.all_gather(received, 'zl', axis=0, tiled=False)  65.6 us
    all_gather x1, blocking collectives, per_device(): lax.all_gather(jnp.sum(residual_cols * residual_cols, axis=1), EXP)  32.9 us
    all_to_all x1, blocking collectives, per_device(): lax.all_to_all(send_rows.reshape(ctx_count, exp_local * capacity, col_wid...  31.6 us
    reduce_scatter x1, waiting for transfers between devices, per_device(): lax.psum_scatter(partial_value, 'c', scatter_dimension=0, tiled=True)[0]  23.2 us
    all_to_all x1, waiting for transfers between devices, per_device(): lax.all_to_all(expert_cols.reshape(ctx_count, capacity, col_width), CTX,...  22.2 us
    all_to_all x1, starting transfers between devices, per_device(): lax.all_to_all(expert_cols.reshape(ctx_count, capacity, col_width), CTX,...  16.9 us
  transfers between devices with their start and end apart: 8, of which 8 were waited for; matrix products, arithmetic and copies ran while one was open for 5% of the time, Pallas kernels for 0%

profile of v1, /device:TPU:32, one launch (start us, length us, event | category | flops | bytes accessed | tf_op | source)
XLA Modules:
  0.0 528.5 jit_solution(15238096650398320670)
XLA Ops:
  11.3 113.0 %all-gather.7.cloned.1.call-done = bf16[4096,128]{0,1:T(8,128)(2,1)} async-done(((bf16[128,128]{0,1:T(8,128)(2,1)}), bf16[4096,128]{0,1:T(8,128)(2,1)}) %all-gather.7.cloned.1.call-update) | async-done | bytes 1048592 | tf_op jit(solution)/shard_map/all_gather | solution.py:108
  124.3 2.0 fusion.45
  127.0 2.1 fusion.13
  131.1 16.4 %reduce-scatter.11.cloned.1.call-done = bf16[1,8,128,180]{2,1,3,0:T(8,128)(2,1)} async-done(((bf16[2,8,128,180]{2,1,3,0:T(8,128)(2,1)}), bf16[1,8,128,180]{2,1,3,0:T(8,128)(2,1)}) %reduce-scatter.11.cloned.1.call-update) | async-done | bytes 368656 | tf_op jit(solution)/shard_map/reduce_scatter | solution.py:134
  153.0 55.7 %reduce-scatter.15.cloned.1.call-done = bf16[1,128,180]{1,2,0:T(8,128)(2,1)} async-done(((bf16[8,128,180]{1,2,0:T(8,128)(2,1)}), bf16[1,128,180]{1,2,0:T(8,128)(2,1)}) %reduce-scatter.15.cloned.1.call-update) | async-done | bytes 46096
  209.7 32.9 %all-gather.2 = f32[16,1,128]{2,1,0:T(1,128)S(1)} all-gather(f32[1,1,128]{2,1,0:T(1,128)S(1)} %bitcast.92), channel_id=2, replica_groups=mesh['zh'=2,'y'=4,'x'=4,'zl'=8,'c'=2] {'zl','c'}, dimensions={0}, use_global_device_ids=true | all-gather | bytes 8704 | tf_op jit(solution)/shard_map/all_gather | solution.py:140
  243.0 2.4 scatter_custom_fusion
  245.5 31.6 %all_to_all.10 = bf16[32,20,180]{2,1,0:T(8,128)(2,1)S(1)} all-to-all(bf16[32,20,180]{2,1,0:T(8,128)(2,1)S(1)} %reshape.316), channel_id=1, replica_groups=mesh['zh'=2,'y'=4,'x'=4,'zl'=8,'c'=2] {'zh','y','x'}, dimensions={0} | all-to-all | bytes 460800 | tf_op jit(solution)/shard_map/all_to_all | solution.py:162
  278.1 65.6 %all-gather.9.cloned.1.call-done = bf16[8,640,180]{1,2,0:T(8,128)(2,1)} async-done(((bf16[1,640,180]{1,2,0:T(8,128)(2,1)}), bf16[8,640,180]{1,2,0:T(8,128)(2,1)}) %all-gather.9.cloned.1.call-update) | async-done | bytes 1843216 | tf_op jit(solution)/shard_map/all_gather | solution.py:169
  343.7 3.0 copy.79
  346.9 1.8 copy.81
  348.8 9.8 %reshape.317 = bf16[8,2,180,360]{2,1,0,3:T(2,128)(2,1)} reshape(bf16[1,2880,2,180]{1,3,2,0:T(8,128)(2,1)S(1)} %copy.81) | data formatting | bytes 4147200 | tf_op jit(solution)/shard_map/reshape | solution.py:171
  358.5 6.4 %reshape.318 = bf16[180,8,2,180]{3,2,1,0:T(2,128)(2,1)S(1)} reshape(bf16[1,180,2880]{2,1,0:T(8,128)(2,1)} %param.23) | data formatting | bytes 2073600 | tf_op jit(solution)/shard_map/reshape | solution.py:181
  364.9 5.6 %all-gather.11.cloned.1.call-done = bf16[16,640,180]{1,0,2:T(8,128)(2,1)} async-done(((bf16[8,640,180]{1,0,2:T(8,128)(2,1)}), bf16[16,640,180]{1,0,2:T(8,128)(2,1)}) %all-gather.11.cloned.1.call-update) | async-done | bytes 3686416 | tf_op jit(solution)/shard_map/all_gather | solution.py:170
  370.6 3.0 copy.80
  373.6 3.0 fusion.8
  376.6 1.8 convert_bitcast_fusion
  378.4 2.6 copy.85
  381.3 23.2 %reduce-scatter.13.cloned.1.call-done = bf16[1,8,640,180]{2,1,3,0:T(8,128)(2,1)} async-done(((bf16[2,8,640,180]{2,1,3,0:T(8,128)(2,1)}), bf16[1,8,640,180]{2,1,3,0:T(8,128)(2,1)}) %reduce-scatter.13.cloned.1.call-update) | async-done | bytes 1843216 | tf_op jit(solution)/shard_map/reduce_scatter | solution.py:185
  404.5 3.0 copy.86
  407.6 69.3 %reduce-scatter.17.cloned.1.call-done = bf16[1,640,180]{1,2,0:T(8,128)(2,1)} async-done(((bf16[8,640,180]{1,2,0:T(8,128)(2,1)}), bf16[1,640,180]{1,2,0:T(8,128)(2,1)}) %reduce-scatter.17.cloned.1.call-update) | async-done | bytes 230416
  478.8 16.9 %all-to-all-start.1 = ((bf16[32,20,180]{2,1,0:T(8,128)(2,1)}), bf16[32,20,180]{2,1,0:T(8,128)(2,1)S(1)}, u32[]{:S(2)}, u32[]{:S(2)}) async-start(bf16[32,20,180]{2,1,0:T(8,128)(2,1)} %reshape_squeeze.3), calls=%async_computation.3 | async-start | bytes 786432 | tf_op jit(solution)/shard_map/all_to_all | solution.py:187
  496.1 22.2 %all-to-all-done.1 = bf16[32,20,180]{2,1,0:T(8,128)(2,1)S(1)} async-done(((bf16[32,20,180]{2,1,0:T(8,128)(2,1)}), bf16[32,20,180]{2,1,0:T(8,128)(2,1)S(1)}, u32[]{:S(2)}, u32[]{:S(2)}) %all-to-all-start.1) | async-done | bytes 230432 | tf_op jit(solution)/shard_map/all_to_all | solution.py:187
  518.4 2.0 gather_fusion
  (85 shorter events, 19.5 us)
Async XLA Ops:
  6.5 122.5 %copy-start = (bf16[128,2880]{0,1:T(8,128)(2,1)S(1)}, bf16[128,2880]{0,1:T(8,128)(2,1)}, u32[]{:S(2)}) copy-start(bf16[128,2880]{0,1:T(8,128)(2,1)} %param.18) | copy-start | bytes 2211844
  6.5 119.7 %copy-start.5 = (f32[2]{0:T(128)S(1)}, f32[2]{0:T(128)}, u32[]{:S(2)}) copy-start(f32[2]{0:T(128)} %param.17) | copy-start | bytes 28
  6.5 117.7 %all-gather.7.cloned.1.call-start = ((), (), s32[]{:S(2)}) async-start(), calls=%async_computation.6 | async-start | bytes 1081344 | tf_op jit(solution)/shard_map/all_gather | solution.py:108
  9.2 138.3 %reduce-scatter.11.cloned.1.call-start = ((), (), s32[]{:S(2)}) async-start(), calls=%async_computation.7 | async-start | bytes 1105920 | tf_op jit(solution)/shard_map/reduce_scatter | solution.py:134
  124.3 2.7 copy-start.2
  129.1 1.6 copy-start.3
  130.7 78.0 %reduce-scatter.15.cloned.1.call-start = ((), (), s32[]{:S(2)}) async-start(), calls=%async_computation.11 | async-start | bytes 423936
  149.3 194.4 %all-gather.9.cloned.1.call-start = ((), (), s32[]{:S(2)}) async-start(), calls=%async_computation.8 | async-start | bytes 2119680 | tf_op jit(solution)/shard_map/all_gather | solution.py:169
  278.1 92.5 %all-gather.11.cloned.1.call-start = ((), (), s32[]{:S(2)}) async-start(), calls=%async_computation.10 | async-start | bytes 5529600 | tf_op jit(solution)/shard_map/all_gather | solution.py:170
  346.7 57.8 %reduce-scatter.13.cloned.1.call-start = ((), (), s32[]{:S(2)}) async-start(), calls=%async_computation.9 | async-start | bytes 5529600 | tf_op jit(solution)/shard_map/reduce_scatter | solution.py:185
  370.6 3.0 copy-start.1
  381.0 95.8 %reduce-scatter.17.cloned.1.call-start = ((), (), s32[]{:S(2)}) async-start(), calls=%async_computation.12 | async-start | bytes 2119680
  404.5 91.4 %copy-start.4 = (f32[128,4]{0,1:T(4,128)S(1)}, f32[128,4]{0,1:T(4,128)}, u32[]{:S(2)}) copy-start(f32[128,4]{0,1:T(4,128)} %param.21) | copy-start | bytes 6148
  478.8 39.4 %all-to-all-start.1 = ((bf16[32,20,180]{2,1,0:T(8,128)(2,1)}), bf16[32,20,180]{2,1,0:T(8,128)(2,1)S(1)}, u32[]{:S(2)}, u32[]{:S(2)}) async-start(bf16[32,20,180]{2,1,0:T(8,128)(2,1)} %reshape_squeeze.3), calls=%async_computation.3 | async-start | bytes 786432 | tf_op jit(solution)/shard_map/all_to_all | solution.py:187
Sparse Core Ops, SparseCore 0:
  11.4 112.7 all-gather.6
  130.8 16.6 reduce-scatter.10
  150.3 58.3 reduce-scatter.14
  278.2 65.4 all-gather.8
  346.8 23.7 all-gather.10
  381.1 23.3 reduce-scatter.12
  407.7 69.1 reduce-scatter.16
